TPU v7x, 32 devices: a whole 2x2x4 slice. The times are simulated.
32 devices in a mesh: groups: 2 (over y), pix: 4 (over z), sub: 2 (over x), inner: 2 (over core).
Axes of the slice: x: 2, y: 2, z: 4, core: 2. Of those that a mesh axis runs over, the one named last changes fastest.
Arguments:
- cube: bfloat16 [20480, 256], P(('groups', 'pix', 'sub', 'inner')), parts along dimension 0, may hold values from -70 to 70
Outputs:
- spectra: bfloat16 [256, 16, 1280], P(('pix', 'sub'), 'groups', 'inner'), parts along dimension 1
There are 2 independent parts, one for each index of `groups`. A program takes and returns all parts, laid end to end along the dimension named above; each array names one. Nothing has to cross between parts.
All inputs are finite; a program needn't handle non-finite values.
Results may differ from a plain program's by a relative error of at most 0.0067.
Values may be sent and summed in bfloat16 or wider, within the bound.
No kernel may reach another device: no remote copies, remote signals or barrier semaphores. Data moves between devices by JAX's collectives and lax.ppermute only.
A program may use at most 64 MiB of HBM per device.

v0:
```python
import math
import jax
import jax.numpy as jnp
from jax import lax
from jax.sharding import PartitionSpec as P

MODES = 32
ITERS = 4


def matmul_high(left, right):
    return jnp.dot(left, right, precision=lax.Precision.HIGHEST)


def leading_modes(gram_matrix, width_count, sweeps):
    mode_basis = jnp.eye(gram_matrix.shape[0], width_count, dtype=jnp.float32)
    for iteration in range(sweeps):
        product = matmul_high(gram_matrix, mode_basis)
        cross_gram = matmul_high(product.T, product)
        lower_factor = jnp.linalg.cholesky(cross_gram)
        mode_basis = jax.scipy.linalg.solve_triangular(lower_factor, product.T, lower=True).T
    return mode_basis


def delay_table(channels):
    middle = channels // 2
    row_index = lax.broadcasted_iota(jnp.int32, (channels, channels), 0)
    col_index = lax.broadcasted_iota(jnp.int32, (channels, channels), 1)
    harmonic = jnp.where(row_index <= middle, row_index, row_index - middle)
    angles = (harmonic * col_index % channels).astype(jnp.float32) * (2.0 * math.pi / channels)
    values = jnp.where(row_index <= middle, jnp.cos(angles), jnp.sin(angles)) / math.sqrt(channels)
    return values.astype(jnp.bfloat16)


def local(cube):
    pixels, channels = cube.shape
    pixel_count = pixels * lax.axis_size(("pix", "sub", "inner"))
    partial_gram = lax.dot_general(
        cube, cube, (((0,), (0,)), ((), ())), preferred_element_type=jnp.float32
    )
    gram_matrix = lax.psum(partial_gram, ("pix", "sub", "inner"))
    gram_matrix = gram_matrix / pixel_count
    mode_basis = leading_modes(gram_matrix, MODES, ITERS)
    modes_b = mode_basis.astype(jnp.bfloat16)
    amplitudes = jnp.dot(cube, modes_b, preferred_element_type=jnp.float32).astype(jnp.bfloat16)
    cleaned = (cube - jnp.dot(amplitudes, modes_b.T, preferred_element_type=jnp.float32)).astype(
        jnp.bfloat16
    )
    table_b = delay_table(channels)
    coefficients = lax.dot_general(
        table_b, cleaned, (((1,), (1,)), ((), ())), preferred_element_type=jnp.float32
    ).astype(jnp.bfloat16)
    spectra = lax.all_to_all(
        coefficients[:, None, :], ("pix", "sub"), split_axis=0, concat_axis=1, tiled=True
    )
    return spectra


def solution(mesh):
    return jax.shard_map(
        local,
        mesh=mesh,
        in_specs=(P(("groups", "pix", "sub", "inner"), None),),
        out_specs=P(("pix", "sub"), "groups", "inner"),
        check_vma=False,
    )
```

profile of v0, /device:TPU:0, one launch (start us, length us, event | category | flops | bytes accessed | tf_op | source)
XLA Modules:
  0.0 160.6 jit_solution(15145366954899768476)
XLA Ops:
  6.5 0.0 all-reduce.2.cloned.1.call-start
  6.5 2.1 %fusion.59 = f32[256,256]{1,0:T(8,128)} fusion(bf16[640,256]{1,0:T(8,128)(2,1)} %param.4), kind=kOutput, calls=%fused_computation.85 | convolution fusion | flops 83886080 | bytes 589824 | tf_op jit(solution)/shard_map/dot_general | solution.py:38
  8.6 0.0 all-reduce.2.cloned.1.call-update
  8.7 94.6 %all-reduce.2.cloned.1.call-done = f32[256,256]{1,0:T(8,128)} async-done(((f32[256,256]{1,0:T(8,128)}), f32[256,256]{1,0:T(8,128)}) %all-reduce.2.cloned.1.call-update) | async-done | bytes 262160 | tf_op jit(solution)/shard_map/psum | solution.py:41
  103.3 0.0 copy-start
  103.3 1.3 fusion.12
  104.6 0.2 fusion.60
  104.7 0.1 copy.13
  104.8 2.9 %cholesky.74 = f32[32,32]{1,0:T(8,128)S(1)} custom-call(f32[32,32]{1,0:T(8,128)S(1)} %fusion.43), custom_call_target="Cholesky" | custom-call | tf_op jit(solution)/shard_map/jit(cholesky)/cholesky | solution.py:20
  107.8 0.6 compare_reduce_fusion.3
  108.4 0.7 fusion.32
  109.1 2.4 %custom-call.8 = f32[1,32,32]{1,2,0:T(8,128)S(1)} custom-call(f32[1,32,32]{2,1,0:T(8,128)S(1)} %fusion.32), custom_call_target="InvertDiagBlocksLowerTriangular" | custom-call | tf_op jit(solution)/shard_map/jit(_solve_triangular)/triangular_solve | solution.py:21
  111.5 0.2 fusion.30
  111.8 0.0 copy-done
  111.8 0.3 fusion.10
  112.1 0.2 fusion.61
  112.3 0.1 copy.14
  112.4 2.9 %cholesky.85 = f32[32,32]{1,0:T(8,128)S(1)} custom-call(f32[32,32]{1,0:T(8,128)S(1)} %fusion.41), custom_call_target="Cholesky" | custom-call | tf_op jit(solution)/shard_map/jit(cholesky)/cholesky | solution.py:20
  115.3 0.6 compare_reduce_fusion.2
  116.0 0.7 fusion.33
  116.6 2.4 %custom-call.9 = f32[1,32,32]{1,2,0:T(8,128)S(1)} custom-call(f32[1,32,32]{2,1,0:T(8,128)S(1)} %fusion.33), custom_call_target="InvertDiagBlocksLowerTriangular" | custom-call | tf_op jit(solution)/shard_map/jit(_solve_triangular)/triangular_solve | solution.py:21
  119.1 0.2 fusion.28
  119.3 0.3 fusion.8
  119.7 0.2 fusion.62
  119.8 0.1 copy.15
  119.9 2.9 %cholesky.96 = f32[32,32]{1,0:T(8,128)S(1)} custom-call(f32[32,32]{1,0:T(8,128)S(1)} %fusion.39), custom_call_target="Cholesky" | custom-call | tf_op jit(solution)/shard_map/jit(cholesky)/cholesky | solution.py:20
  122.9 0.6 compare_reduce_fusion.1
  123.5 0.7 fusion.34
  124.2 2.4 %custom-call.10 = f32[1,32,32]{1,2,0:T(8,128)S(1)} custom-call(f32[1,32,32]{2,1,0:T(8,128)S(1)} %fusion.34), custom_call_target="InvertDiagBlocksLowerTriangular" | custom-call | tf_op jit(solution)/shard_map/jit(_solve_triangular)/triangular_solve | solution.py:21
  126.6 0.0 copy-start.1
  126.6 0.2 fusion.26
  126.9 0.3 fusion.6
  127.2 0.2 fusion.63
  127.4 0.1 copy.16
  127.5 2.9 %cholesky.107 = f32[32,32]{1,0:T(8,128)S(1)} custom-call(f32[32,32]{1,0:T(8,128)S(1)} %fusion.37), custom_call_target="Cholesky" | custom-call | tf_op jit(solution)/shard_map/jit(cholesky)/cholesky | solution.py:20
  130.4 0.6 compare_reduce_fusion
  131.1 0.7 fusion.35
  131.7 2.4 %custom-call.11 = f32[1,32,32]{1,2,0:T(8,128)S(1)} custom-call(f32[1,32,32]{2,1,0:T(8,128)S(1)} %fusion.35), custom_call_target="InvertDiagBlocksLowerTriangular" | custom-call | tf_op jit(solution)/shard_map/jit(_solve_triangular)/triangular_solve | solution.py:21
  134.2 0.2 convolution_convert_fusion.2
  134.4 0.0 copy-done.1
  134.4 0.2 convolution_convert_fusion.1
  134.6 1.5 fusion.1
  136.1 0.5 broadcast.63
  136.6 0.8 reduce.4
  137.5 0.1 reshape.8
  137.6 15.0 %all_to_all.18 = bf16[8,2,10240]{2,1,0:T(2,128)(2,1)S(1)} all-to-all(bf16[8,2,10240]{2,1,0:T(2,128)(2,1)S(1)} %reshape.8), channel_id=1, replica_groups=mesh['groups'=2,'pix'=4,'sub'=2,'inner'=2] {'pix','sub'}, dimensions={0} | all-to-all | bytes 655360 | tf_op jit(solution)/shard_map/all_to_all | solution.py:53
  152.5 0.3 reshape.9
  152.9 0.8 copy.18
  (11 shorter events, 0.2 us)
Async XLA Ops:
  6.5 96.7 %all-reduce.2.cloned.1.call-start = ((), (), s32[]{:S(2)}) async-start(), calls=%async_computation.1 | async-start | bytes 524288 | tf_op jit(solution)/shard_map/psum | solution.py:41
  103.3 8.5 %copy-start = (f32[256,256]{1,0:T(8,128)S(1)}, f32[256,256]{1,0:T(8,128)}, u32[]{:S(2)}) copy-start(f32[256,256]{1,0:T(8,128)} %all-reduce.2.cloned.1.call-done) | copy-start | bytes 786436
  126.6 7.8 %copy-start.1 = (bf16[640,256]{1,0:T(8,128)(2,1)S(1)}, bf16[640,256]{1,0:T(8,128)(2,1)}, u32[]{:S(2)}) copy-start(bf16[640,256]{1,0:T(8,128)(2,1)} %param.4) | copy-start | bytes 983044
Sparse Core Ops, SparseCore 0:
  10.7 92.4 all-reduce.1
where the time goes:
time: 161 us
  waiting for transfers between devices  94.6 us (59%)
  other arithmetic  27.6 us (17%)
  blocking collectives  15 us (9%)
  between operations  13.6 us (8%)
  matrix products  7.73 us (5%)
  local copies, waits for them, and re-layouts  2.08 us (1%)
    psum x1, waiting for transfers between devices, local(): gram_matrix = lax.psum(partial_gram, ('pix', 'sub', 'inner'))  94.6 us
    all_to_all x1, blocking collectives, local(): lax.all_to_all(coefficients[:, None, :], ('pix', 'sub'), split_axis=0, co...  15 us
    another operation x12, other arithmetic, leading_modes(): lower_factor = jnp.linalg.cholesky(cross_gram)  14.4 us
    another operation x8, other arithmetic, leading_modes(): jax.scipy.linalg.solve_triangular(lower_factor, product.T, lower=True)  12.3 us
  transfers between devices with their start and end apart: 1, of which 1 were waited for; matrix products, arithmetic and copies ran while one was open for 0% of the time, Pallas kernels for 0%

commit v1 on v0

--- a/solution.py
+++ b/solution.py
@@ -38,7 +38,7 @@
     partial_gram = lax.dot_general(
         cube, cube, (((0,), (0,)), ((), ())), preferred_element_type=jnp.float32
     )
-    gram_matrix = lax.psum(partial_gram, ("pix", "sub", "inner"))
+    gram_matrix = jnp.sum(lax.all_gather(partial_gram, ("pix", "sub", "inner")), axis=0)
     gram_matrix = gram_matrix / pixel_count
     mode_basis = leading_modes(gram_matrix, MODES, ITERS)
     modes_b = mode_basis.astype(jnp.bfloat16)

time: 161 us -> 121 us (0.75)
  waiting for transfers between devices: 94.6 us -> 53.9 us
  other arithmetic: 27.6 us -> 30.1 us
    psum x1 -> x0, waiting for transfers between devices: 94.6 us -> none  [local(): gram_matrix = lax.psum(partial_gram, ('pix', 'sub', 'inner'))]
    all_gather x0 -> x1, waiting for transfers between devices: none -> 53.9 us  [local(): lax.all_gather(partial_gram, ('pix', 'sub', 'inner'))]
    reduce_sum x0 -> x1, other arithmetic: none -> 2.48 us  [local(): jnp.sum(lax.all_gather(partial_gram, ('pix', 'sub', 'inner')), axis=0)]
where the time goes in v1:
time: 121 us
  waiting for transfers between devices  53.9 us (45%)
  other arithmetic  30.1 us (25%)
  blocking collectives  14.3 us (12%)
  between operations  13.6 us (11%)
  matrix products  6.76 us (6%)
  local copies, waits for them, and re-layouts  2.07 us (2%)
    all_gather x1, waiting for transfers between devices, local(): lax.all_gather(partial_gram, ('pix', 'sub', 'inner'))  53.9 us
    another operation x12, other arithmetic, leading_modes(): lower_factor = jnp.linalg.cholesky(cross_gram)  14.4 us
    all_to_all x1, blocking collectives, local(): lax.all_to_all(coefficients[:, None, :], ('pix', 'sub'), split_axis=0, co...  14.3 us
    another operation x8, other arithmetic, leading_modes(): jax.scipy.linalg.solve_triangular(lower_factor, product.T, lower=True)  12.3 us
    reduce_sum x1, other arithmetic, local(): jnp.sum(lax.all_gather(partial_gram, ('pix', 'sub', 'inner')), axis=0)  2.48 us
  transfers between devices with their start and end apart: 1, of which 1 were waited for; matrix products, arithmetic and copies ran while one was open for 0% of the time, Pallas kernels for 0%

profile of v1, /device:TPU:0, one launch (start us, length us, event | category | flops | bytes accessed | tf_op | source)
XLA Modules:
  0.0 120.7 jit_solution(13079681372410257915)
XLA Ops:
  6.5 0.0 copy-start
  6.5 0.0 all-gather.3.cloned.1.call-start
  6.5 2.1 %fusion.59 = f32[256,256]{1,0:T(8,128)} fusion(bf16[640,256]{1,0:T(8,128)(2,1)} %param.4), kind=kOutput, calls=%fused_computation.85 | convolution fusion | flops 83886080 | bytes 589824 | tf_op jit(solution)/shard_map/dot_general | solution.py:38
  8.7 0.0 all-gather.3.cloned.1.call-update
  8.7 53.9 %all-gather.3.cloned.1.call-done = f32[4096,256]{1,0:T(8,128)} async-done(((f32[256,256]{1,0:T(8,128)}), f32[4096,256]{1,0:T(8,128)}) %all-gather.3.cloned.1.call-update) | async-done | bytes 4194320 | tf_op jit(solution)/shard_map/all_gather | solution.py:41
  62.6 2.5 %reduce_sum.9 = f32[256,256]{1,0:T(8,128)S(1)} reduce(f32[16,256,256]{2,1,0:T(8,128)} %bitcast.73, f32[]{:T(128)} %constant.58.clone.1), dimensions={0}, to_apply=%region_0.0 | reduce | flops 983040 | bytes 4456452 | tf_op jit(solution)/shard_map/reduce_sum | solution.py:41
  65.1 0.3 fusion.12
  65.4 0.2 fusion.60
  65.5 0.1 copy.13
  65.6 2.9 %cholesky.74 = f32[32,32]{1,0:T(8,128)S(1)} custom-call(f32[32,32]{1,0:T(8,128)S(1)} %fusion.43), custom_call_target="Cholesky" | custom-call | tf_op jit(solution)/shard_map/jit(cholesky)/cholesky | solution.py:20
  68.6 0.6 compare_reduce_fusion.3
  69.2 0.7 fusion.32
  69.9 2.4 %custom-call.8 = f32[1,32,32]{1,2,0:T(8,128)S(1)} custom-call(f32[1,32,32]{2,1,0:T(8,128)S(1)} %fusion.32), custom_call_target="InvertDiagBlocksLowerTriangular" | custom-call | tf_op jit(solution)/shard_map/jit(_solve_triangular)/triangular_solve | solution.py:21
  72.3 0.2 fusion.30
  72.6 0.3 fusion.10
  72.9 0.2 fusion.61
  73.1 0.1 copy.14
  73.2 2.9 %cholesky.85 = f32[32,32]{1,0:T(8,128)S(1)} custom-call(f32[32,32]{1,0:T(8,128)S(1)} %fusion.41), custom_call_target="Cholesky" | custom-call | tf_op jit(solution)/shard_map/jit(cholesky)/cholesky | solution.py:20
  76.1 0.6 compare_reduce_fusion.2
  76.8 0.7 fusion.33
  77.4 2.4 %custom-call.9 = f32[1,32,32]{1,2,0:T(8,128)S(1)} custom-call(f32[1,32,32]{2,1,0:T(8,128)S(1)} %fusion.33), custom_call_target="InvertDiagBlocksLowerTriangular" | custom-call | tf_op jit(solution)/shard_map/jit(_solve_triangular)/triangular_solve | solution.py:21
  79.9 0.2 fusion.28
  80.1 0.3 fusion.8
  80.5 0.2 fusion.62
  80.6 0.1 copy.15
  80.7 2.9 %cholesky.96 = f32[32,32]{1,0:T(8,128)S(1)} custom-call(f32[32,32]{1,0:T(8,128)S(1)} %fusion.39), custom_call_target="Cholesky" | custom-call | tf_op jit(solution)/shard_map/jit(cholesky)/cholesky | solution.py:20
  83.7 0.6 compare_reduce_fusion.1
  84.3 0.7 fusion.34
  85.0 2.4 %custom-call.10 = f32[1,32,32]{1,2,0:T(8,128)S(1)} custom-call(f32[1,32,32]{2,1,0:T(8,128)S(1)} %fusion.34), custom_call_target="InvertDiagBlocksLowerTriangular" | custom-call | tf_op jit(solution)/shard_map/jit(_solve_triangular)/triangular_solve | solution.py:21
  87.4 0.2 fusion.26
  87.7 0.3 fusion.6
  88.0 0.2 fusion.63
  88.2 0.1 copy.16
  88.3 2.9 %cholesky.107 = f32[32,32]{1,0:T(8,128)S(1)} custom-call(f32[32,32]{1,0:T(8,128)S(1)} %fusion.37), custom_call_target="Cholesky" | custom-call | tf_op jit(solution)/shard_map/jit(cholesky)/cholesky | solution.py:20
  91.2 0.6 compare_reduce_fusion
  91.9 0.7 fusion.35
  92.5 2.4 %custom-call.11 = f32[1,32,32]{1,2,0:T(8,128)S(1)} custom-call(f32[1,32,32]{2,1,0:T(8,128)S(1)} %fusion.35), custom_call_target="InvertDiagBlocksLowerTriangular" | custom-call | tf_op jit(solution)/shard_map/jit(_solve_triangular)/triangular_solve | solution.py:21
  95.0 0.2 convolution_convert_fusion.2
  95.2 0.0 copy-done
  95.2 0.2 convolution_convert_fusion.1
  95.4 1.5 %fusion.1 = bf16[256,1,640]{2,0,1:T(8,128)(2,1)S(1)} fusion(bf16[32,640]{1,0:T(8,128)(2,1)S(1)} %convolution_convert_fusion.1, bf16[32,256]{1,0:T(8,128)(2,1)S(1)} %convolution_convert_fusion.2, bf16[640,256]{1,0:T(8,128)(2,1)S(1)} %copy-done, s32[256]{0:T(256)S(1)} %iota_add_fusion, pred[256]{0:T(512)(128)(4,1)S(1)} %iota_compare_fusion.4), kind=kOutput, calls=%fused_computation.3 | convolution fusion | flops 96206848 | bytes 713984 | tf_op jit(solution)/shard_map/dot_general | solution.py:50
  96.9 0.5 broadcast.63
  97.4 0.8 reduce.4
  98.3 0.1 reshape.9
  98.4 14.3 %all_to_all.18 = bf16[8,2,10240]{2,1,0:T(2,128)(2,1)S(1)} all-to-all(bf16[8,2,10240]{2,1,0:T(2,128)(2,1)S(1)} %reshape.9), channel_id=1, replica_groups=mesh['groups'=2,'pix'=4,'sub'=2,'inner'=2] {'pix','sub'}, dimensions={0} | all-to-all | bytes 655360 | tf_op jit(solution)/shard_map/all_to_all | solution.py:53
  112.6 0.3 reshape.10
  113.0 0.8 copy.18
  (11 shorter events, 0.2 us)
Async XLA Ops:
  6.5 88.7 %copy-start = (bf16[640,256]{1,0:T(8,128)(2,1)S(1)}, bf16[640,256]{1,0:T(8,128)(2,1)}, u32[]{:S(2)}) copy-start(bf16[640,256]{1,0:T(8,128)(2,1)} %param.4) | copy-start | bytes 983044
  6.5 56.1 %all-gather.3.cloned.1.call-start = ((), (), s32[]{:S(2)}) async-start(), calls=%async_computation.1 | async-start | bytes 4456448 | tf_op jit(solution)/shard_map/all_gather | solution.py:41
Sparse Core Ops, SparseCore 0:
  9.5 53.0 all-gather.2
